TPU v7x, 512 devices: a whole 4x8x8 slice. The times are simulated.
512 devices in a mesh: doc: 16 (over z_lo, y), label: 32 (over x, z_hi, core).
Axes of the slice: x: 4, y: 8, z: 8 (z_hi: 4, z_lo: 2; z = z_hi * 2 + z_lo), core: 2. Of those that a mesh axis runs over, the one named last changes fastest.
Arguments:
- doc_embed: bfloat16 [16384, 768], P(('doc', 'label')), may hold values from -0.59765625 to 0.59765625
- classifier: bfloat16 [32768, 768], P('label'), may hold values from -4.28125 to 4.28125
- centroids: bfloat16 [256, 768], P('doc'), may hold values from -4.28125 to 4.28125
- shortlist: int32 [16384, 32], P(('doc', 'label')), may hold values from 0 to 255, all different within a row
- positives: int32 [16384, 4], P(('doc', 'label')), may hold values from 0 to 4095
Outputs:
- grad_classifier: bfloat16 [32768, 768], P('label')
- grad_centroids: float32 [256, 768], P('doc')
- grad_docs: bfloat16 [16384, 768], P(('doc', 'label'))
Inputs may be any that keep to these rules, and one draw needn't show every extreme that they name: `shortlist`: each row names 32 different clusters; every cluster is named by some row.
All inputs are finite; a program needn't handle non-finite values.
Results may differ from a plain program's by a relative error of at most 0.015.
Values may be sent and summed in bfloat16 or wider, within the bound.
No kernel may reach another device: no remote copies, remote signals or barrier semaphores. Data moves between devices by JAX's collectives and lax.ppermute only.
A program may use at most 64 MiB of HBM per device.

v0:
```python
import jax
import jax.numpy as jnp
from jax import lax
from jax.sharding import PartitionSpec as P

CLS = 128
LOSS_WEIGHT = 0.125


def tile_grads(rows, short_rows, pos_rows, classifier, cent_rows, cluster_base):
    labels_dev = classifier.shape[0]
    local_clusters = cluster_base + jnp.arange(labels_dev // CLS, dtype=jnp.int32)
    local_labels = cluster_base * CLS + jnp.arange(labels_dev, dtype=jnp.int32)
    logits = jnp.einsum("nd,ld->nl", rows, classifier, preferred_element_type=jnp.float32)
    member = jnp.any(short_rows[:, :, None] == local_clusters[None, None, :], axis=1)
    mask = jnp.repeat(member, CLS, axis=1)
    target = jnp.any(pos_rows[:, :, None] == local_labels[None, None, :], axis=1)
    grad = (
        LOSS_WEIGHT
        * (jax.nn.sigmoid(logits) - target.astype(jnp.float32))
        * mask.astype(jnp.float32)
    ).astype(jnp.bfloat16)
    meta_logits = jnp.einsum("nd,cd->nc", rows, cent_rows, preferred_element_type=jnp.float32)
    pos_clusters = pos_rows // CLS
    meta_target = jnp.any(pos_clusters[:, :, None] == local_clusters[None, None, :], axis=1)
    meta_grad = (
        LOSS_WEIGHT * (jax.nn.sigmoid(meta_logits) - meta_target.astype(jnp.float32))
    ).astype(jnp.bfloat16)
    return (grad, meta_grad)


def body(doc_embed, classifier, centroids, shortlist, positives):
    labels_dev = classifier.shape[0]
    cl_here = labels_dev // CLS
    per_doc = centroids.shape[0]
    label_index = lax.axis_index("label")
    cluster_base = label_index * cl_here
    pos_cluster = jnp.take_along_axis(shortlist, positives // CLS, axis=1)
    pos_label = pos_cluster * CLS + positives % CLS
    all_cent = lax.all_gather(centroids, "doc", axis=0, tiled=True)
    cent_rows = lax.dynamic_slice_in_dim(all_cent, cluster_base, cl_here, 0)
    rows, short_rows, pos_rows = (
        lax.all_gather(doc_embed, "label", axis=0, tiled=True),
        lax.all_gather(shortlist, "label", axis=0, tiled=True),
        lax.all_gather(pos_label, "label", axis=0, tiled=True),
    )
    grad, meta_grad = tile_grads(rows, short_rows, pos_rows, classifier, cent_rows, cluster_base)
    class_acc = jnp.einsum("nl,nd->ld", grad, rows, preferred_element_type=jnp.float32)
    cent_acc = jnp.einsum("nc,nd->cd", meta_grad, rows, preferred_element_type=jnp.float32)
    input_sum = lax.psum_scatter(
        (
            jnp.dot(grad, classifier, preferred_element_type=jnp.float32)
            + jnp.dot(meta_grad, cent_rows, preferred_element_type=jnp.float32)
        ).astype(jnp.bfloat16),
        "label",
        scatter_dimension=0,
        tiled=True,
    )
    grad_classifier = lax.psum(class_acc.astype(jnp.bfloat16), "doc")
    cent_summed = lax.psum(cent_acc, "doc")
    cent_whole = lax.all_gather(cent_summed, "label", axis=0, tiled=True)
    grad_centroids = lax.dynamic_slice_in_dim(
        cent_whole, lax.axis_index("doc") * per_doc, per_doc, 0
    )
    return (grad_classifier, grad_centroids, input_sum)


def solution(mesh):
    in_specs = (
        P(("doc", "label"), None),
        P("label", None),
        P("doc", None),
        P(("doc", "label"), None),
        P(("doc", "label"), None),
    )
    out_specs = (P("label", None), P("doc", None), P(("doc", "label"), None))
    return jax.shard_map(body, mesh=mesh, in_specs=in_specs, out_specs=out_specs, check_vma=False)
```

profile of v0, /device:TPU:8, one launch (start us, length us, event | category | flops | bytes accessed | tf_op | source)
XLA Modules:
  0.0 373.3 jit_solution(2617783042345759563)
XLA Ops:
  7.2 0.0 all-gather.3.cloned.1.call-start
  7.2 0.7 all-gather.3.cloned.1.call-update
  7.9 0.0 all-reduce.2.cloned.1.call-start
  8.0 0.7 bitcast_or_fusion
  8.7 0.1 copy.47
  8.8 0.1 reshape.31
  8.9 1.3 gather_fusion
  10.2 0.1 reshape.34
  10.3 0.1 copy.48
  10.4 50.2 %all-gather = s32[32,32,4]{1,2,0:T(4,128)S(1)} all-gather(s32[1,32,4]{1,2,0:T(4,128)S(1)} %fusion.12), channel_id=1, replica_groups=mesh['doc'=16,'label'=32] {'label'}, dimensions={0}, use_global_device_ids=true | all-gather | bytes 16896 | tf_op jit(solution)/shard_map/all_gather | solution.py:45
  60.6 0.1 reshape.43
  60.7 41.3 %all_gather.15 = s32[1024,32]{1,0:T(8,128)S(1)} all-gather(s32[32,32]{1,0:T(8,128)S(1)} %copy-done.1), channel_id=1, replica_groups=mesh['doc'=16,'label'=32] {'label'}, dimensions={0}, use_global_device_ids=true | all-gather | bytes 135168 | tf_op jit(solution)/shard_map/all_gather | solution.py:44
  102.1 0.2 copy.45
  102.2 0.2 compare_reduce_fusion.1
  102.5 0.3 copy.46
  102.7 3.8 %compare_reduce_fusion = pred[1024,1024]{1,0:T(8,128)(4,1)} fusion(s32[1024]{0:T(1024)S(1)} %iota_add_fusion, s32[1024,4]{0,1:T(4,128)S(1)} %reshape.43), kind=kLoop, calls=%fused_computation.1 | loop fusion | flops 7340032 | bytes 1069056 | tf_op jit(solution)/shard_map/reduce_or | solution.py:17
  106.6 3.2 broadcast_in_dim.6
  109.7 4.6 %select_convert_fusion = bf16[1024,1024]{1,0:T(8,128)(2,1)S(1)} fusion(pred[1024,1024]{1,0:T(8,128)(4,1)} %compare_reduce_fusion, pred[128,8,8,128]{3,2,1,0:T(8,128)(4,1)S(1)} %bitcast.29, bf16[1024,768]{1,0:T(8,128)(2,1)} %all-gather.3.cloned.1.call-done, bf16[1024,768]{1,0:T(8,128)(2,1)S(1)} %copy-done), kind=kOutput, calls=%fused_computation.2 | convolution fusion | flops 1619001344 | bytes 7340032 | tf_op jit(solution)/shard_map/nd,ld->nl/dot_general | solution.py:14
  114.3 1.3 copy-done.5
  115.7 3.0 convolution_convert_fusion
  118.7 0.0 reduce-scatter.2.cloned.1.call-start
  118.8 0.1 compare_reduce_fusion.2
  118.9 35.4 %all_gather.18 = bf16[256,768]{1,0:T(8,128)(2,1)S(1)} all-gather(bf16[16,768]{1,0:T(8,128)(2,1)S(1)} %copy-done.3), channel_id=1, replica_groups=mesh['doc'=16,'label'=32] {'doc'}, dimensions={0}, use_global_device_ids=true | all-gather | bytes 417792 | tf_op jit(solution)/shard_map/all_gather | solution.py:40
  154.3 0.5 fusion.6
  154.8 3.4 fusion.17
  158.2 1.8 add_convert_fusion
  160.1 0.3 fusion.16
  160.4 59.2 %psum.15 = f32[8,768]{1,0:T(8,128)S(1)} all-reduce(f32[8,768]{1,0:T(8,128)S(1)} %fusion.16), channel_id=1, replica_groups=mesh['doc'=16,'label'=32] {'doc'}, use_global_device_ids=true, to_apply=%region_4.5 | all-reduce | flops 6144 | bytes 49152 | tf_op jit(solution)/shard_map/psum | solution.py:60
  219.6 44.9 %all_gather.19 = f32[256,768]{1,0:T(8,128)S(1)} all-gather(f32[8,768]{1,0:T(8,128)S(1)} %psum.15), channel_id=1, replica_groups=mesh['doc'=16,'label'=32] {'label'}, dimensions={0}, use_global_device_ids=true | all-gather | bytes 811008 | tf_op jit(solution)/shard_map/all_gather | solution.py:61
  264.5 0.6 constant_dynamic-slice_fusion
  265.1 99.0 %reduce-scatter.2.cloned.1.call-done = bf16[32,768]{1,0:T(8,128)(2,1)} async-done(((bf16[1024,768]{1,0:T(8,128)(2,1)}), bf16[32,768]{1,0:T(8,128)(2,1)}) %reduce-scatter.2.cloned.1.call-update) | async-done | bytes 49168 | tf_op jit(solution)/shard_map/reduce_scatter | solution.py:50
  364.1 2.7 copy.53
  (20 shorter events, 0.1 us)
Async XLA Ops:
  7.2 102.6 %copy-start = (bf16[1024,768]{1,0:T(8,128)(2,1)S(1)}, bf16[1024,768]{1,0:T(8,128)(2,1)}, u32[]{:S(2)}) copy-start(bf16[1024,768]{1,0:T(8,128)(2,1)} %param.6) | copy-start | bytes 4718596
  7.2 1.7 copy-start.1
  7.2 99.4 %all-gather.3.cloned.1.call-start = ((), (), s32[]{:S(2)}) async-start(), calls=%async_computation.1 | async-start | bytes 1622016 | tf_op jit(solution)/shard_map/all_gather | solution.py:43
  7.9 257.2 %all-reduce.2.cloned.1.call-start = ((), (), s32[]{:S(2)}) async-start(), calls=%async_computation.2 | async-start | bytes 3145728 | tf_op jit(solution)/shard_map/psum | solution.py:59
  8.9 1.5 copy-start.4
  109.7 5.9 %copy-start.2 = (bf16[1024,768]{1,0:T(8,128)(2,1)S(1)}, bf16[1024,768]{1,0:T(8,128)(2,1)}, u32[]{:S(2)}) copy-start(bf16[1024,768]{1,0:T(8,128)(2,1)} %all-gather.3.cloned.1.call-done) | copy-start | bytes 4718596
  114.3 1.4 copy-start.5
  115.7 3.2 copy-start.3
  118.7 245.4 %reduce-scatter.2.cloned.1.call-start = ((), (), s32[]{:S(2)}) async-start(), calls=%async_computation.3 | async-start | bytes 1622016 | tf_op jit(solution)/shard_map/reduce_scatter | solution.py:50
Sparse Core Ops, SparseCore 0:
  11.1 64.0 all-gather.2
  118.9 141.9 all-reduce.1
  265.9 98.2 reduce-scatter.1
where the time goes:
time: 374 us; the launch traced here: 373 us
  blocking collectives  231 us (62%)
  waiting for transfers between devices  99.7 us (27%)
  between operations  13.9 us (4%)
  matrix products  13.6 us (4%)
  local copies, waits for them, and re-layouts  9.97 us (3%)
  other arithmetic  4.87 us (1%)
    reduce_scatter x1, waiting for transfers between devices, body(): lax.psum_scatter((jnp.dot(grad, classifier, preferred_element_type=jnp.fl...  99 us
    psum x1, blocking collectives, body(): cent_summed = lax.psum(cent_acc, 'doc')  59.2 us
    all_gather x1, blocking collectives, body(): lax.all_gather(pos_label, 'label', axis=0, tiled=True)  50.2 us
    all_gather x1, blocking collectives, body(): cent_whole = lax.all_gather(cent_summed, 'label', axis=0, tiled=True)  44.9 us
    all_gather x1, blocking collectives, body(): lax.all_gather(shortlist, 'label', axis=0, tiled=True)  41.3 us
    all_gather x1, blocking collectives, body(): all_cent = lax.all_gather(centroids, 'doc', axis=0, tiled=True)  35.4 us
  transfers between devices with their start and end apart: 3, of which 1 were waited for; matrix products, arithmetic and copies ran while one was open for 4% of the time, Pallas kernels for 0%

commit v1 on v0

--- a/solution.py
+++ b/solution.py
@@ -1,3 +1,4 @@
+import functools
 import jax
 import jax.numpy as jnp
 from jax import lax
@@ -5,6 +6,17 @@
 
 CLS = 128
 LOSS_WEIGHT = 0.125
+
+
+def connect_counts(block_here, peer_axis):
+    answer = lax.axis_size(peer_axis)
+    plain = jnp.stack([block_here] * answer, axis=0)
+    arr_now = lax.all_to_all(plain, peer_axis, 0, 0)
+    right_arr = jnp.concatenate(arr_now, 0)
+    return right_arr
+
+
+handle_racks = functools.partial(connect_counts, peer_axis="label")
 
 
 def tile_grads(rows, short_rows, pos_rows, classifier, cent_rows, cluster_base):
@@ -42,7 +54,7 @@
     rows, short_rows, pos_rows = (
         lax.all_gather(doc_embed, "label", axis=0, tiled=True),
         lax.all_gather(shortlist, "label", axis=0, tiled=True),
-        lax.all_gather(pos_label, "label", axis=0, tiled=True),
+        handle_racks(pos_label),
     )
     grad, meta_grad = tile_grads(rows, short_rows, pos_rows, classifier, cent_rows, cluster_base)
     class_acc = jnp.einsum("nl,nd->ld", grad, rows, preferred_element_type=jnp.float32)

time: 374 us -> 342 us (0.914)
  blocking collectives: 231 us -> 183 us
  starting transfers between devices: 0.12 us -> 13.3 us
    all_gather x1 -> x0, blocking collectives: 50.2 us -> none  [body(): lax.all_gather(pos_label, 'label', axis=0, tiled=True)]
    all_to_all x0 -> x1, starting transfers between devices: none -> 13.2 us  [connect_counts(): arr_now = lax.all_to_all(plain, peer_axis, 0, 0)]
    all_gather x1, blocking collectives: 41.3 us -> 47.2 us  [body(): lax.all_gather(shortlist, 'label', axis=0, tiled=True)]
    all_gather x1, blocking collectives: 44.9 us -> 41.1 us  [body(): cent_whole = lax.all_gather(cent_summed, 'label', axis=0, tiled=True)]
  transfers between devices with their start and end apart: 3 -> 4, of which waited for: 1 -> 1; matrix products, arithmetic and copies ran while one was open for 4% -> 5% of each run, Pallas kernels for 0% -> 0%
where the time goes in v1:
time: 342 us
  blocking collectives  183 us (54%)
  waiting for transfers between devices  101 us (30%)
  between operations  14 us (4%)
  matrix products  13.6 us (4%)
  starting transfers between devices  13.3 us (4%)
  local copies, waits for them, and re-layouts  11.3 us (3%)
  other arithmetic  5.54 us (2%)
    reduce_scatter x1, waiting for transfers between devices, body(): lax.psum_scatter((jnp.dot(grad, classifier, preferred_element_type=jnp.fl...  100 us
    psum x1, blocking collectives, body(): cent_summed = lax.psum(cent_acc, 'doc')  60.4 us
    all_gather x1, blocking collectives, body(): lax.all_gather(shortlist, 'label', axis=0, tiled=True)  47.2 us
    all_gather x1, blocking collectives, body(): cent_whole = lax.all_gather(cent_summed, 'label', axis=0, tiled=True)  41.1 us
    all_gather x1, blocking collectives, body(): all_cent = lax.all_gather(centroids, 'doc', axis=0, tiled=True)  34.5 us
    all_to_all x1, starting transfers between devices, connect_counts(): arr_now = lax.all_to_all(plain, peer_axis, 0, 0)  13.2 us
  transfers between devices with their start and end apart: 4, of which 1 were waited for; matrix products, arithmetic and copies ran while one was open for 5% of the time, Pallas kernels for 0%

profile of v1, /device:TPU:8, one launch (start us, length us, event | category | flops | bytes accessed | tf_op | source)
XLA Modules:
  0.0 342.1 jit_solution(1461167035357559620)
XLA Ops:
  7.2 0.7 all-gather.2.cloned.1.call-update
  7.9 0.7 bitcast_or_fusion
  8.6 0.1 copy.49
  8.7 0.1 reshape.61
  8.8 1.3 gather_fusion
  10.1 0.1 reshape.64
  10.4 0.7 reshape.72
  11.1 13.2 %all-to-all-start = ((s32[32,1,128]{2,1,0:T(1,128)}), s32[32,1,128]{2,1,0:T(1,128)S(1)}, u32[]{:S(2)}, u32[]{:S(2)}) async-start(s32[32,1,128]{2,1,0:T(1,128)} %reshape.72), calls=%async_computation | async-start | bytes 32768 | tf_op jit(solution)/shard_map/all_to_all | solution.py:14
  24.3 47.2 %all_gather.12 = s32[1024,32]{1,0:T(8,128)S(1)} all-gather(s32[32,32]{1,0:T(8,128)S(1)} %copy-done.1), channel_id=1, replica_groups=mesh['doc'=16,'label'=32] {'label'}, dimensions={0}, use_global_device_ids=true | all-gather | bytes 135168 | tf_op jit(solution)/shard_map/all_gather | solution.py:56
  71.5 0.2 copy.47
  71.6 0.2 compare_reduce_fusion.1
  71.9 0.3 copy.48
  72.2 0.5 broadcast.117
  72.7 0.7 reduce
  73.4 0.1 reshape.73
  73.5 0.1 eq.46
  73.6 3.8 %compare_reduce_fusion = pred[1024,1024]{1,0:T(8,128)(4,1)} fusion(s32[1024]{0:T(1024)S(1)} %iota_add_fusion, s32[1024,4]{0,1:T(4,128)S(1)} %eq.46), kind=kLoop, calls=%fused_computation.1 | loop fusion | flops 7340032 | bytes 1069056 | tf_op jit(solution)/shard_map/reduce_or | solution.py:29
  77.4 3.2 broadcast_in_dim.6
  80.6 4.5 %select_convert_fusion = bf16[1024,1024]{1,0:T(8,128)(2,1)S(1)} fusion(pred[1024,1024]{1,0:T(8,128)(4,1)} %compare_reduce_fusion, pred[128,8,8,128]{3,2,1,0:T(8,128)(4,1)S(1)} %bitcast.30, bf16[1024,768]{1,0:T(8,128)(2,1)} %all-gather.2.cloned.1.call-done, bf16[1024,768]{1,0:T(8,128)(2,1)S(1)} %copy-done), kind=kOutput, calls=%fused_computation.2 | convolution fusion | flops 1619001344 | bytes 7340032 | tf_op jit(solution)/shard_map/nd,ld->nl/dot_general | solution.py:26
  85.1 1.3 copy-done.5
  86.5 3.0 convolution_convert_fusion
  89.6 34.5 %all_gather.14 = bf16[256,768]{1,0:T(8,128)(2,1)S(1)} all-gather(bf16[16,768]{1,0:T(8,128)(2,1)S(1)} %copy-done.3), channel_id=1, replica_groups=mesh['doc'=16,'label'=32] {'doc'}, dimensions={0}, use_global_device_ids=true | all-gather | bytes 417792 | tf_op jit(solution)/shard_map/all_gather | solution.py:52
  124.1 0.1 compare_reduce_fusion.2
  124.2 0.5 fusion.6
  124.7 3.4 fusion.16
  128.1 1.8 add_convert_fusion
  130.0 0.3 fusion.15
  130.3 60.4 %psum.15 = f32[8,768]{1,0:T(8,128)S(1)} all-reduce(f32[8,768]{1,0:T(8,128)S(1)} %fusion.15), channel_id=1, replica_groups=mesh['doc'=16,'label'=32] {'doc'}, use_global_device_ids=true, to_apply=%region_4.5 | all-reduce | flops 6144 | bytes 49152 | tf_op jit(solution)/shard_map/psum | solution.py:72
  190.7 41.1 %all_gather.15 = f32[256,768]{1,0:T(8,128)S(1)} all-gather(f32[8,768]{1,0:T(8,128)S(1)} %psum.15), channel_id=1, replica_groups=mesh['doc'=16,'label'=32] {'label'}, dimensions={0}, use_global_device_ids=true | all-gather | bytes 811008 | tf_op jit(solution)/shard_map/all_gather | solution.py:73
  231.8 0.6 constant_dynamic-slice_fusion
  232.5 100.5 %reduce-scatter.2.cloned.1.call-done = bf16[32,768]{1,0:T(8,128)(2,1)} async-done(((bf16[1024,768]{1,0:T(8,128)(2,1)}), bf16[32,768]{1,0:T(8,128)(2,1)}) %reduce-scatter.2.cloned.1.call-update) | async-done | bytes 49168 | tf_op jit(solution)/shard_map/reduce_scatter | solution.py:62
  333.0 2.7 copy.55
  (26 shorter events, 0.3 us)
Async XLA Ops:
  7.2 73.4 %copy-start = (bf16[1024,768]{1,0:T(8,128)(2,1)S(1)}, bf16[1024,768]{1,0:T(8,128)(2,1)}, u32[]{:S(2)}) copy-start(bf16[1024,768]{1,0:T(8,128)(2,1)} %param.6) | copy-start | bytes 4718596
  7.2 1.6 copy-start.1
  7.2 70.2 %all-gather.2.cloned.1.call-start = ((), (), s32[]{:S(2)}) async-start(), calls=%async_computation.2 | async-start | bytes 1622016 | tf_op jit(solution)/shard_map/all_gather | solution.py:55
  8.8 1.5 copy-start.4
  11.1 61.1 %all-to-all-start = ((s32[32,1,128]{2,1,0:T(1,128)}), s32[32,1,128]{2,1,0:T(1,128)S(1)}, u32[]{:S(2)}, u32[]{:S(2)}) async-start(s32[32,1,128]{2,1,0:T(1,128)} %reshape.72), calls=%async_computation | async-start | bytes 32768 | tf_op jit(solution)/shard_map/all_to_all | solution.py:14
  24.2 208.2 %all-reduce.2.cloned.1.call-start = ((), (), s32[]{:S(2)}) async-start(), calls=%async_computation.3 | async-start | bytes 3145728 | tf_op jit(solution)/shard_map/psum | solution.py:71
  80.6 5.9 %copy-start.2 = (bf16[1024,768]{1,0:T(8,128)(2,1)S(1)}, bf16[1024,768]{1,0:T(8,128)(2,1)}, u32[]{:S(2)}) copy-start(bf16[1024,768]{1,0:T(8,128)(2,1)} %all-gather.2.cloned.1.call-done) | copy-start | bytes 4718596
  85.1 1.4 copy-start.5
  86.5 3.1 copy-start.3
  89.6 243.4 %reduce-scatter.2.cloned.1.call-start = ((), (), s32[]{:S(2)}) async-start(), calls=%async_computation.4 | async-start | bytes 1622016 | tf_op jit(solution)/shard_map/reduce_scatter | solution.py:62
Sparse Core Ops, SparseCore 0:
  11.1 63.6 all-gather.1
  89.7 140.2 all-reduce.1
  235.0 97.9 reduce-scatter.1
